TPU v7x, 128 devices: a whole 4x4x4 slice. The times are simulated.
128 devices in a mesh: row: 64 (over z, y, x), col: 2 (over core).
Axes of the slice: x: 4, y: 4, z: 4, core: 2. Of those that a mesh axis runs over, the one named last changes fastest.
Arguments:
- basis: bfloat16 [512, 64, 512], P('row', 'col'), may hold values from -0.25 to 0.25
- positions: float32 [512, 3, 512], P('row'), may hold values from 0 to 1
- seglen: float32 [512, 512], P('row'), may hold values from 0.5 to 2
- radius: float32 [512, 512], P('row'), may hold values from 0.05 to 0.2
- neighbours: int32 [512, 16], P('row'), may hold values from 0 to 511, as said below
- counts: int32 [512], P('row'), may hold values from 1 to 16, as said below
Outputs:
- reduced: float32 [512, 64, 1024], P('row', 'col')
Inputs may be any that keep to these rules, and one draw needn't show every extreme that they name: `neighbours`: each neighbour index differs from its own block's index by at most 8; slot 0 always differs by exactly 8. `counts`: the first block of every 8 has all 16 slots live.
All inputs are finite; a program needn't handle non-finite values.
Results may differ from a plain program's by a relative error of at most 0.019.
Values may be sent and summed in bfloat16 or wider, within the bound.
No kernel may reach another device: no remote copies, remote signals or barrier semaphores. Data moves between devices by JAX's collectives and lax.ppermute only.
A program may use at most 64 MiB of HBM per device.

v0:
```python
import jax
import jax.numpy as jnp
from jax import lax
from jax.sharding import PartitionSpec as P


def extended(block, sides, width):
    for axis, dim in sides:
        count = lax.axis_size(axis)
        forward = [(i, i + 1) for i in range(count - 1)]
        backward = [(target, source) for source, target in forward]
        low = lax.ppermute(
            lax.slice_in_dim(block, block.shape[dim] - width, None, axis=dim), axis, forward
        )
        high = lax.ppermute(lax.slice_in_dim(block, 0, width, axis=dim), axis, backward)
        block = jnp.concatenate([low, block, high], axis=dim)
    return block


def on_device(basis, positions, seglen, radius, neighbours, counts):
    blk_local = basis.shape[0]
    first_block = lax.axis_index("row") * blk_local - blk_local
    whole_own = lax.all_gather(basis, "col", axis=1, tiled=True)
    ext_panels, ext_pos, ext_len, ext_rad = (
        extended(whole_own, (("row", 0),), blk_local),
        extended(positions.astype(jnp.bfloat16), (("row", 0),), blk_local).astype(positions.dtype),
        extended(seglen.astype(jnp.bfloat16), (("row", 0),), blk_local).astype(seglen.dtype),
        extended(radius.astype(jnp.bfloat16), (("row", 0),), blk_local).astype(radius.dtype),
    )
    unknowns = positions.shape[2]
    window = ext_panels.shape[0]
    geometry = jnp.concatenate((ext_pos.reshape(window, 3 * unknowns), ext_len, ext_rad), axis=1)
    slot_ids = jnp.transpose(neighbours - first_block)
    slot_live = jnp.arange(neighbours.shape[1], dtype=jnp.int32)[:, None] < counts[None, :]
    window_ids = jnp.arange(window, dtype=jnp.int32)

    def one_slot(items):
        local_ids, live = items
        picker = local_ids[:, None] == window_ids[None, :]
        geo_near = jnp.dot(
            picker.astype(jnp.float32),
            geometry,
            precision=lax.Precision.HIGHEST,
            preferred_element_type=jnp.float32,
        )
        pos_near = geo_near[:, : 3 * unknowns].reshape(blk_local, 3, unknowns)
        len_near = geo_near[:, 3 * unknowns : 4 * unknowns]
        rad_near = geo_near[:, 4 * unknowns :]
        dist_sq = jnp.zeros((blk_local, unknowns, unknowns), jnp.float32)
        for coord in range(3):
            gap = positions[:, coord][:, :, None] - pos_near[:, coord][:, None, :]
            dist_sq = dist_sq + gap * gap
        coupling = (
            seglen[:, :, None]
            * len_near[:, None, :]
            / jnp.sqrt(dist_sq + radius[:, :, None] * rad_near[:, None, :])
        )
        coupling = coupling.astype(jnp.bfloat16)
        left = jnp.einsum(
            "bpm,bmn->bpn", basis, coupling, preferred_element_type=jnp.float32
        ).astype(jnp.bfloat16)
        panels = jnp.einsum(
            "bj,jqn->bqn",
            picker.astype(jnp.bfloat16),
            ext_panels,
            preferred_element_type=jnp.float32,
        ).astype(jnp.bfloat16)
        tiles = jnp.einsum("bpn,bqn->bpq", left, panels, preferred_element_type=jnp.float32)
        return tiles * live.astype(jnp.float32)[:, None, None]

    stacked = lax.map(one_slot, (slot_ids, slot_live))
    result = jnp.transpose(stacked, (1, 2, 0, 3)).reshape(blk_local, stacked.shape[2], -1)
    return result


def solution(mesh):
    placed = (
        P("row", "col", None),
        P("row", None, None),
        P("row", None),
        P("row", None),
        P("row", None),
        P("row"),
    )
    return jax.shard_map(
        on_device, mesh=mesh, in_specs=placed, out_specs=P("row", "col", None), check_vma=False
    )
```

profile of v0, /device:TPU:30, one launch (start us, length us, event | category | flops | bytes accessed | tf_op | source)
XLA Modules:
  0.0 163.4 jit_solution(2376370793642495294)
XLA Ops:
  0.0 0.8 convert_element_type.35
  0.8 3.4 %collective-permute-start = (bf16[8,3,512]{2,0,1:T(8,128)(2,1)S(1)}, bf16[8,3,512]{2,0,1:T(8,128)(2,1)S(1)}, u32[]{:S(2)}, u32[]{:S(2)}) collective-permute-start(bf16[8,3,512]{2,0,1:T(8,128)(2,1)S(1)} %convert_element_type.35), channel_id=1, source_target_pairs={{0,2},{2,4},{4,6},{6,8},{8,10},{10,12},{12,14},{14,16},{16,18},{18... | collective-permute-start | bytes 73736 | tf_op jit(solution)/shard_map/ppermute | solution.py:12
  4.2 2.4 %collective-permute-start.1 = (bf16[8,3,512]{2,0,1:T(8,128)(2,1)S(1)}, bf16[8,3,512]{2,0,1:T(8,128)(2,1)S(1)}, u32[]{:S(2)}, u32[]{:S(2)}) collective-permute-start(bf16[8,3,512]{2,0,1:T(8,128)(2,1)S(1)} %convert_element_type.35), channel_id=1, source_target_pairs={{2,0},{4,2},{6,4},{8,6},{10,8},{12,10},{14,12},{16,14},{18,16},{20... | collective-permute-start | bytes 73736 | tf_op jit(solution)/shard_map/ppermute | solution.py:15
  6.7 0.7 convert_element_type.36
  7.4 7.6 %collective-permute-start.2 = (bf16[8,512]{1,0:T(8,128)(2,1)S(1)}, bf16[8,512]{1,0:T(8,128)(2,1)S(1)}, u32[]{:S(2)}, u32[]{:S(2)}) collective-permute-start(bf16[8,512]{1,0:T(8,128)(2,1)S(1)} %convert_element_type.36), channel_id=1, source_target_pairs={{0,2},{2,4},{4,6},{6,8},{8,10},{10,12},{12,14},{14,16},{16,18},{18... | collective-permute-start | bytes 24584 | tf_op jit(solution)/shard_map/ppermute | solution.py:12
  15.0 1.9 %collective-permute-start.3 = (bf16[8,512]{1,0:T(8,128)(2,1)S(1)}, bf16[8,512]{1,0:T(8,128)(2,1)S(1)}, u32[]{:S(2)}, u32[]{:S(2)}) collective-permute-start(bf16[8,512]{1,0:T(8,128)(2,1)S(1)} %convert_element_type.36), channel_id=1, source_target_pairs={{2,0},{4,2},{6,4},{8,6},{10,8},{12,10},{14,12},{16,14},{18,16},{20... | collective-permute-start | bytes 24584 | tf_op jit(solution)/shard_map/ppermute | solution.py:15
  17.6 8.1 %collective-permute-start.4 = (bf16[8,512]{1,0:T(8,128)(2,1)S(1)}, bf16[8,512]{1,0:T(8,128)(2,1)S(1)}, u32[]{:S(2)}, u32[]{:S(2)}) collective-permute-start(bf16[8,512]{1,0:T(8,128)(2,1)S(1)} %convert_element_type.37), channel_id=1, source_target_pairs={{0,2},{2,4},{4,6},{6,8},{8,10},{10,12},{12,14},{14,16},{16,18},{18... | collective-permute-start | bytes 24584 | tf_op jit(solution)/shard_map/ppermute | solution.py:12
  26.5 2.5 %all_gather.3 = bf16[8,64,512]{2,1,0:T(8,128)(2,1)S(1)} all-gather(bf16[8,32,512]{2,1,0:T(8,128)(2,1)} %param.8), channel_id=1, replica_groups=mesh['row'=64,'col'=2] {'col'}, dimensions={1}, use_global_device_ids=true | all-gather | bytes 786432 | tf_op jit(solution)/shard_map/all_gather | solution.py:23
  29.0 1.9 %collective-permute-start.5 = (bf16[8,512]{1,0:T(8,128)(2,1)S(1)}, bf16[8,512]{1,0:T(8,128)(2,1)S(1)}, u32[]{:S(2)}, u32[]{:S(2)}) collective-permute-start(bf16[8,512]{1,0:T(8,128)(2,1)S(1)} %convert_element_type.37), channel_id=1, source_target_pairs={{2,0},{4,2},{6,4},{8,6},{10,8},{12,10},{14,12},{16,14},{18,16},{20... | collective-permute-start | bytes 24584 | tf_op jit(solution)/shard_map/ppermute | solution.py:15
  30.9 8.1 %collective-permute-start.6 = (bf16[8,64,512]{2,1,0:T(8,128)(2,1)S(1)}, bf16[8,64,512]{2,1,0:T(8,128)(2,1)S(1)}, u32[]{:S(2)}, u32[]{:S(2)}) collective-permute-start(bf16[8,64,512]{2,1,0:T(8,128)(2,1)S(1)} %all_gather.3), channel_id=1, source_target_pairs={{0,2},{2,4},{4,6},{6,8},{8,10},{10,12},{12,14},{14,16},{16,18},{18... | collective-permute-start | bytes 1572872 | tf_op jit(solution)/shard_map/ppermute | solution.py:12
  39.1 1.9 %collective-permute-start.7 = (bf16[8,64,512]{2,1,0:T(8,128)(2,1)S(1)}, bf16[8,64,512]{2,1,0:T(8,128)(2,1)S(1)}, u32[]{:S(2)}, u32[]{:S(2)}) collective-permute-start(bf16[8,64,512]{2,1,0:T(8,128)(2,1)S(1)} %all_gather.3), channel_id=1, source_target_pairs={{2,0},{4,2},{6,4},{8,6},{10,8},{12,10},{14,12},{16,14},{18,16},{20... | collective-permute-start | bytes 1572872 | tf_op jit(solution)/shard_map/ppermute | solution.py:15
  41.8 8.5 %collective-permute-done.6 = bf16[8,64,512]{2,1,0:T(8,128)(2,1)S(1)} collective-permute-done((bf16[8,64,512]{2,1,0:T(8,128)(2,1)S(1)}, bf16[8,64,512]{2,1,0:T(8,128)(2,1)S(1)}, u32[]{:S(2)}, u32[]{:S(2)}) %collective-permute-start.6) | collective-permute-done | bytes 524320 | tf_op jit(solution)/shard_map/ppermute | solution.py:12
  50.3 8.3 %collective-permute-done.7 = bf16[8,64,512]{2,1,0:T(8,128)(2,1)S(1)} collective-permute-done((bf16[8,64,512]{2,1,0:T(8,128)(2,1)S(1)}, bf16[8,64,512]{2,1,0:T(8,128)(2,1)S(1)}, u32[]{:S(2)}, u32[]{:S(2)}) %collective-permute-start.7) | collective-permute-done | bytes 524320 | tf_op jit(solution)/shard_map/ppermute | solution.py:15
  58.8 100.3 %while.11 = (s32[]{:T(128)}, f32[16,8,32,64]{3,2,1,0:T(8,128)}, f32[8,512]{1,0:T(8,128)S(1)}, s32[16,8]{1,0:T(8,128)S(1)}, f32[24,2560]{1,0:T(8,128)S(1)}, /*ind...) while((s32[]{:T(128)}, f32[16,8,32,64]{3,2,1,0:T(8,128)}, ...), condition=%wide.region_1.2_spmd.clone, body=%wide.region_0.1_spmd.clone.sunk | while | flops 196886912 | bytes 4916057 | solution.py:71
  59.1 1.2 fusion.35
  60.3 4.8 %fusion.37 = f32[16,8,32,64]{3,2,1,0:T(8,128)} fusion(f32[16,8,32,64]{3,2,1,0:T(8,128)} %get-tuple-element.215, s32[]{:T(128)} %get-tuple-element.214, bf16[8,32,512]{2,1,0:T(8,128)(2,1)S(1)} %copy-done.1, f32[8,512]{1,0:T(8,128)S(1)} %get-tuple-element.195, f32[8,512]{1,0:T(8,128)S(1)} %get-tuple-element.231, f32[8,512]{1,0:T(8,128)S(1)} %get-tuple-element.196, ...), kind=kOutput, calls=%fused_computation.8.clone.1 | convolution fusion | flops 178405376 | bytes 1081888 | tf_op jit(solution)/shard_map/while/body/eval_jaxpr/bpn,bqn->bpq/dot_general | solution.py:68
  65.4 1.2 fusion.35
  66.6 4.8 %fusion.37 = f32[16,8,32,64]{3,2,1,0:T(8,128)} fusion(f32[16,8,32,64]{3,2,1,0:T(8,128)} %get-tuple-element.215, s32[]{:T(128)} %get-tuple-element.214, bf16[8,32,512]{2,1,0:T(8,128)(2,1)S(1)} %copy-done.1, f32[8,512]{1,0:T(8,128)S(1)} %get-tuple-element.195, f32[8,512]{1,0:T(8,128)S(1)} %get-tuple-element.231, f32[8,512]{1,0:T(8,128)S(1)} %get-tuple-element.196, ...), kind=kOutput, calls=%fused_computation.8.clone.1 | convolution fusion | flops 178405376 | bytes 1081888 | tf_op jit(solution)/shard_map/while/body/eval_jaxpr/bpn,bqn->bpq/dot_general | solution.py:68
  71.7 1.2 fusion.35
  72.9 4.8 %fusion.37 = f32[16,8,32,64]{3,2,1,0:T(8,128)} fusion(f32[16,8,32,64]{3,2,1,0:T(8,128)} %get-tuple-element.215, s32[]{:T(128)} %get-tuple-element.214, bf16[8,32,512]{2,1,0:T(8,128)(2,1)S(1)} %copy-done.1, f32[8,512]{1,0:T(8,128)S(1)} %get-tuple-element.195, f32[8,512]{1,0:T(8,128)S(1)} %get-tuple-element.231, f32[8,512]{1,0:T(8,128)S(1)} %get-tuple-element.196, ...), kind=kOutput, calls=%fused_computation.8.clone.1 | convolution fusion | flops 178405376 | bytes 1081888 | tf_op jit(solution)/shard_map/while/body/eval_jaxpr/bpn,bqn->bpq/dot_general | solution.py:68
  77.9 1.2 fusion.35
  79.1 4.8 %fusion.37 = f32[16,8,32,64]{3,2,1,0:T(8,128)} fusion(f32[16,8,32,64]{3,2,1,0:T(8,128)} %get-tuple-element.215, s32[]{:T(128)} %get-tuple-element.214, bf16[8,32,512]{2,1,0:T(8,128)(2,1)S(1)} %copy-done.1, f32[8,512]{1,0:T(8,128)S(1)} %get-tuple-element.195, f32[8,512]{1,0:T(8,128)S(1)} %get-tuple-element.231, f32[8,512]{1,0:T(8,128)S(1)} %get-tuple-element.196, ...), kind=kOutput, calls=%fused_computation.8.clone.1 | convolution fusion | flops 178405376 | bytes 1081888 | tf_op jit(solution)/shard_map/while/body/eval_jaxpr/bpn,bqn->bpq/dot_general | solution.py:68
  84.2 1.2 fusion.35
  85.4 4.8 %fusion.37 = f32[16,8,32,64]{3,2,1,0:T(8,128)} fusion(f32[16,8,32,64]{3,2,1,0:T(8,128)} %get-tuple-element.215, s32[]{:T(128)} %get-tuple-element.214, bf16[8,32,512]{2,1,0:T(8,128)(2,1)S(1)} %copy-done.1, f32[8,512]{1,0:T(8,128)S(1)} %get-tuple-element.195, f32[8,512]{1,0:T(8,128)S(1)} %get-tuple-element.231, f32[8,512]{1,0:T(8,128)S(1)} %get-tuple-element.196, ...), kind=kOutput, calls=%fused_computation.8.clone.1 | convolution fusion | flops 178405376 | bytes 1081888 | tf_op jit(solution)/shard_map/while/body/eval_jaxpr/bpn,bqn->bpq/dot_general | solution.py:68
  90.4 1.2 fusion.35
  91.6 4.8 %fusion.37 = f32[16,8,32,64]{3,2,1,0:T(8,128)} fusion(f32[16,8,32,64]{3,2,1,0:T(8,128)} %get-tuple-element.215, s32[]{:T(128)} %get-tuple-element.214, bf16[8,32,512]{2,1,0:T(8,128)(2,1)S(1)} %copy-done.1, f32[8,512]{1,0:T(8,128)S(1)} %get-tuple-element.195, f32[8,512]{1,0:T(8,128)S(1)} %get-tuple-element.231, f32[8,512]{1,0:T(8,128)S(1)} %get-tuple-element.196, ...), kind=kOutput, calls=%fused_computation.8.clone.1 | convolution fusion | flops 178405376 | bytes 1081888 | tf_op jit(solution)/shard_map/while/body/eval_jaxpr/bpn,bqn->bpq/dot_general | solution.py:68
  96.7 1.2 fusion.35
  97.9 4.8 %fusion.37 = f32[16,8,32,64]{3,2,1,0:T(8,128)} fusion(f32[16,8,32,64]{3,2,1,0:T(8,128)} %get-tuple-element.215, s32[]{:T(128)} %get-tuple-element.214, bf16[8,32,512]{2,1,0:T(8,128)(2,1)S(1)} %copy-done.1, f32[8,512]{1,0:T(8,128)S(1)} %get-tuple-element.195, f32[8,512]{1,0:T(8,128)S(1)} %get-tuple-element.231, f32[8,512]{1,0:T(8,128)S(1)} %get-tuple-element.196, ...), kind=kOutput, calls=%fused_computation.8.clone.1 | convolution fusion | flops 178405376 | bytes 1081888 | tf_op jit(solution)/shard_map/while/body/eval_jaxpr/bpn,bqn->bpq/dot_general | solution.py:68
  103.0 1.2 fusion.35
  104.2 4.8 %fusion.37 = f32[16,8,32,64]{3,2,1,0:T(8,128)} fusion(f32[16,8,32,64]{3,2,1,0:T(8,128)} %get-tuple-element.215, s32[]{:T(128)} %get-tuple-element.214, bf16[8,32,512]{2,1,0:T(8,128)(2,1)S(1)} %copy-done.1, f32[8,512]{1,0:T(8,128)S(1)} %get-tuple-element.195, f32[8,512]{1,0:T(8,128)S(1)} %get-tuple-element.231, f32[8,512]{1,0:T(8,128)S(1)} %get-tuple-element.196, ...), kind=kOutput, calls=%fused_computation.8.clone.1 | convolution fusion | flops 178405376 | bytes 1081888 | tf_op jit(solution)/shard_map/while/body/eval_jaxpr/bpn,bqn->bpq/dot_general | solution.py:68
  109.2 1.2 fusion.35
  110.4 4.8 %fusion.37 = f32[16,8,32,64]{3,2,1,0:T(8,128)} fusion(f32[16,8,32,64]{3,2,1,0:T(8,128)} %get-tuple-element.215, s32[]{:T(128)} %get-tuple-element.214, bf16[8,32,512]{2,1,0:T(8,128)(2,1)S(1)} %copy-done.1, f32[8,512]{1,0:T(8,128)S(1)} %get-tuple-element.195, f32[8,512]{1,0:T(8,128)S(1)} %get-tuple-element.231, f32[8,512]{1,0:T(8,128)S(1)} %get-tuple-element.196, ...), kind=kOutput, calls=%fused_computation.8.clone.1 | convolution fusion | flops 178405376 | bytes 1081888 | tf_op jit(solution)/shard_map/while/body/eval_jaxpr/bpn,bqn->bpq/dot_general | solution.py:68
  115.5 1.2 fusion.35
  116.7 4.8 %fusion.37 = f32[16,8,32,64]{3,2,1,0:T(8,128)} fusion(f32[16,8,32,64]{3,2,1,0:T(8,128)} %get-tuple-element.215, s32[]{:T(128)} %get-tuple-element.214, bf16[8,32,512]{2,1,0:T(8,128)(2,1)S(1)} %copy-done.1, f32[8,512]{1,0:T(8,128)S(1)} %get-tuple-element.195, f32[8,512]{1,0:T(8,128)S(1)} %get-tuple-element.231, f32[8,512]{1,0:T(8,128)S(1)} %get-tuple-element.196, ...), kind=kOutput, calls=%fused_computation.8.clone.1 | convolution fusion | flops 178405376 | bytes 1081888 | tf_op jit(solution)/shard_map/while/body/eval_jaxpr/bpn,bqn->bpq/dot_general | solution.py:68
  121.8 1.2 fusion.35
  123.0 4.8 %fusion.37 = f32[16,8,32,64]{3,2,1,0:T(8,128)} fusion(f32[16,8,32,64]{3,2,1,0:T(8,128)} %get-tuple-element.215, s32[]{:T(128)} %get-tuple-element.214, bf16[8,32,512]{2,1,0:T(8,128)(2,1)S(1)} %copy-done.1, f32[8,512]{1,0:T(8,128)S(1)} %get-tuple-element.195, f32[8,512]{1,0:T(8,128)S(1)} %get-tuple-element.231, f32[8,512]{1,0:T(8,128)S(1)} %get-tuple-element.196, ...), kind=kOutput, calls=%fused_computation.8.clone.1 | convolution fusion | flops 178405376 | bytes 1081888 | tf_op jit(solution)/shard_map/while/body/eval_jaxpr/bpn,bqn->bpq/dot_general | solution.py:68
  128.0 1.2 fusion.35
  129.2 4.8 %fusion.37 = f32[16,8,32,64]{3,2,1,0:T(8,128)} fusion(f32[16,8,32,64]{3,2,1,0:T(8,128)} %get-tuple-element.215, s32[]{:T(128)} %get-tuple-element.214, bf16[8,32,512]{2,1,0:T(8,128)(2,1)S(1)} %copy-done.1, f32[8,512]{1,0:T(8,128)S(1)} %get-tuple-element.195, f32[8,512]{1,0:T(8,128)S(1)} %get-tuple-element.231, f32[8,512]{1,0:T(8,128)S(1)} %get-tuple-element.196, ...), kind=kOutput, calls=%fused_computation.8.clone.1 | convolution fusion | flops 178405376 | bytes 1081888 | tf_op jit(solution)/shard_map/while/body/eval_jaxpr/bpn,bqn->bpq/dot_general | solution.py:68
  134.3 1.2 fusion.35
  135.5 4.8 %fusion.37 = f32[16,8,32,64]{3,2,1,0:T(8,128)} fusion(f32[16,8,32,64]{3,2,1,0:T(8,128)} %get-tuple-element.215, s32[]{:T(128)} %get-tuple-element.214, bf16[8,32,512]{2,1,0:T(8,128)(2,1)S(1)} %copy-done.1, f32[8,512]{1,0:T(8,128)S(1)} %get-tuple-element.195, f32[8,512]{1,0:T(8,128)S(1)} %get-tuple-element.231, f32[8,512]{1,0:T(8,128)S(1)} %get-tuple-element.196, ...), kind=kOutput, calls=%fused_computation.8.clone.1 | convolution fusion | flops 178405376 | bytes 1081888 | tf_op jit(solution)/shard_map/while/body/eval_jaxpr/bpn,bqn->bpq/dot_general | solution.py:68
  140.5 1.2 fusion.35
  141.7 4.8 %fusion.37 = f32[16,8,32,64]{3,2,1,0:T(8,128)} fusion(f32[16,8,32,64]{3,2,1,0:T(8,128)} %get-tuple-element.215, s32[]{:T(128)} %get-tuple-element.214, bf16[8,32,512]{2,1,0:T(8,128)(2,1)S(1)} %copy-done.1, f32[8,512]{1,0:T(8,128)S(1)} %get-tuple-element.195, f32[8,512]{1,0:T(8,128)S(1)} %get-tuple-element.231, f32[8,512]{1,0:T(8,128)S(1)} %get-tuple-element.196, ...), kind=kOutput, calls=%fused_computation.8.clone.1 | convolution fusion | flops 178405376 | bytes 1081888 | tf_op jit(solution)/shard_map/while/body/eval_jaxpr/bpn,bqn->bpq/dot_general | solution.py:68
  146.8 1.2 fusion.35
  148.0 4.8 %fusion.37 = f32[16,8,32,64]{3,2,1,0:T(8,128)} fusion(f32[16,8,32,64]{3,2,1,0:T(8,128)} %get-tuple-element.215, s32[]{:T(128)} %get-tuple-element.214, bf16[8,32,512]{2,1,0:T(8,128)(2,1)S(1)} %copy-done.1, f32[8,512]{1,0:T(8,128)S(1)} %get-tuple-element.195, f32[8,512]{1,0:T(8,128)S(1)} %get-tuple-element.231, f32[8,512]{1,0:T(8,128)S(1)} %get-tuple-element.196, ...), kind=kOutput, calls=%fused_computation.8.clone.1 | convolution fusion | flops 178405376 | bytes 1081888 | tf_op jit(solution)/shard_map/while/body/eval_jaxpr/bpn,bqn->bpq/dot_general | solution.py:68
  153.1 1.2 fusion.35
  154.3 4.8 %fusion.37 = f32[16,8,32,64]{3,2,1,0:T(8,128)} fusion(f32[16,8,32,64]{3,2,1,0:T(8,128)} %get-tuple-element.215, s32[]{:T(128)} %get-tuple-element.214, bf16[8,32,512]{2,1,0:T(8,128)(2,1)S(1)} %copy-done.1, f32[8,512]{1,0:T(8,128)S(1)} %get-tuple-element.195, f32[8,512]{1,0:T(8,128)S(1)} %get-tuple-element.231, f32[8,512]{1,0:T(8,128)S(1)} %get-tuple-element.196, ...), kind=kOutput, calls=%fused_computation.8.clone.1 | convolution fusion | flops 178405376 | bytes 1081888 | tf_op jit(solution)/shard_map/while/body/eval_jaxpr/bpn,bqn->bpq/dot_general | solution.py:68
  159.1 2.8 %copy.10 = f32[8,32,16,64]{3,2,1,0:T(8,128)S(1)} copy(f32[8,32,16,64]{3,1,0,2:T(8,128)} %bitcast.51) | data formatting | bytes 2097152 | tf_op jit(solution)/shard_map/transpose | solution.py:72
  161.9 1.5 reshape.28
  (147 shorter events, 6.8 us)
Async XLA Ops:
  0.8 41.0 %collective-permute-start = (bf16[8,3,512]{2,0,1:T(8,128)(2,1)S(1)}, bf16[8,3,512]{2,0,1:T(8,128)(2,1)S(1)}, u32[]{:S(2)}, u32[]{:S(2)}) collective-permute-start(bf16[8,3,512]{2,0,1:T(8,128)(2,1)S(1)} %convert_element_type.35), channel_id=1, source_target_pairs={{0,2},{2,4},{4,6},{6,8},{8,10},{10,12},{12,14},{14,16},{16,18},{18... | collective-permute-start | bytes 73736 | tf_op jit(solution)/shard_map/ppermute | solution.py:12
  4.2 37.6 %collective-permute-start.1 = (bf16[8,3,512]{2,0,1:T(8,128)(2,1)S(1)}, bf16[8,3,512]{2,0,1:T(8,128)(2,1)S(1)}, u32[]{:S(2)}, u32[]{:S(2)}) collective-permute-start(bf16[8,3,512]{2,0,1:T(8,128)(2,1)S(1)} %convert_element_type.35), channel_id=1, source_target_pairs={{2,0},{4,2},{6,4},{8,6},{10,8},{12,10},{14,12},{16,14},{18,16},{20... | collective-permute-start | bytes 73736 | tf_op jit(solution)/shard_map/ppermute | solution.py:15
  7.4 21.6 %collective-permute-start.2 = (bf16[8,512]{1,0:T(8,128)(2,1)S(1)}, bf16[8,512]{1,0:T(8,128)(2,1)S(1)}, u32[]{:S(2)}, u32[]{:S(2)}) collective-permute-start(bf16[8,512]{1,0:T(8,128)(2,1)S(1)} %convert_element_type.36), channel_id=1, source_target_pairs={{0,2},{2,4},{4,6},{6,8},{8,10},{10,12},{12,14},{14,16},{16,18},{18... | collective-permute-start | bytes 24584 | tf_op jit(solution)/shard_map/ppermute | solution.py:12
  15.0 15.9 %collective-permute-start.3 = (bf16[8,512]{1,0:T(8,128)(2,1)S(1)}, bf16[8,512]{1,0:T(8,128)(2,1)S(1)}, u32[]{:S(2)}, u32[]{:S(2)}) collective-permute-start(bf16[8,512]{1,0:T(8,128)(2,1)S(1)} %convert_element_type.36), channel_id=1, source_target_pairs={{2,0},{4,2},{6,4},{8,6},{10,8},{12,10},{14,12},{16,14},{18,16},{20... | collective-permute-start | bytes 24584 | tf_op jit(solution)/shard_map/ppermute | solution.py:15
  17.6 21.4 %collective-permute-start.4 = (bf16[8,512]{1,0:T(8,128)(2,1)S(1)}, bf16[8,512]{1,0:T(8,128)(2,1)S(1)}, u32[]{:S(2)}, u32[]{:S(2)}) collective-permute-start(bf16[8,512]{1,0:T(8,128)(2,1)S(1)} %convert_element_type.37), channel_id=1, source_target_pairs={{0,2},{2,4},{4,6},{6,8},{8,10},{10,12},{12,14},{14,16},{16,18},{18... | collective-permute-start | bytes 24584 | tf_op jit(solution)/shard_map/ppermute | solution.py:12
  26.5 32.3 %copy-start = (f32[8,3,512]{2,0,1:T(8,128)S(1)}, f32[8,3,512]{2,0,1:T(8,128)}, u32[]{:S(2)}) copy-start(f32[8,3,512]{2,0,1:T(8,128)} %param.9) | copy-start | bytes 147460
  26.5 32.3 %copy-start.2 = (f32[8,512]{1,0:T(8,128)S(1)}, f32[8,512]{1,0:T(8,128)}, u32[]{:S(2)}) copy-start(f32[8,512]{1,0:T(8,128)} %param.10) | copy-start | bytes 49156
  26.5 32.3 %copy-start.3 = (f32[8,512]{1,0:T(8,128)S(1)}, f32[8,512]{1,0:T(8,128)}, u32[]{:S(2)}) copy-start(f32[8,512]{1,0:T(8,128)} %param.11) | copy-start | bytes 49156
  29.0 12.8 %collective-permute-start.5 = (bf16[8,512]{1,0:T(8,128)(2,1)S(1)}, bf16[8,512]{1,0:T(8,128)(2,1)S(1)}, u32[]{:S(2)}, u32[]{:S(2)}) collective-permute-start(bf16[8,512]{1,0:T(8,128)(2,1)S(1)} %convert_element_type.37), channel_id=1, source_target_pairs={{2,0},{4,2},{6,4},{8,6},{10,8},{12,10},{14,12},{16,14},{18,16},{20... | collective-permute-start | bytes 24584 | tf_op jit(solution)/shard_map/ppermute | solution.py:15
  30.9 19.3 %collective-permute-start.6 = (bf16[8,64,512]{2,1,0:T(8,128)(2,1)S(1)}, bf16[8,64,512]{2,1,0:T(8,128)(2,1)S(1)}, u32[]{:S(2)}, u32[]{:S(2)}) collective-permute-start(bf16[8,64,512]{2,1,0:T(8,128)(2,1)S(1)} %all_gather.3), channel_id=1, source_target_pairs={{0,2},{2,4},{4,6},{6,8},{8,10},{10,12},{12,14},{14,16},{16,18},{18... | collective-permute-start | bytes 1572872 | tf_op jit(solution)/shard_map/ppermute | solution.py:12
  39.1 19.5 %collective-permute-start.7 = (bf16[8,64,512]{2,1,0:T(8,128)(2,1)S(1)}, bf16[8,64,512]{2,1,0:T(8,128)(2,1)S(1)}, u32[]{:S(2)}, u32[]{:S(2)}) collective-permute-start(bf16[8,64,512]{2,1,0:T(8,128)(2,1)S(1)} %all_gather.3), channel_id=1, source_target_pairs={{2,0},{4,2},{6,4},{8,6},{10,8},{12,10},{14,12},{16,14},{18,16},{20... | collective-permute-start | bytes 1572872 | tf_op jit(solution)/shard_map/ppermute | solution.py:15
  58.8 1.5 copy-start.1
  65.1 1.5 copy-start.1
  71.4 1.5 copy-start.1
  77.6 1.5 copy-start.1
  83.9 1.5 copy-start.1
  90.1 1.5 copy-start.1
  96.4 1.5 copy-start.1
  102.7 1.5 copy-start.1
  108.9 1.5 copy-start.1
  115.2 1.5 copy-start.1
  121.5 1.5 copy-start.1
  127.7 1.5 copy-start.1
  134.0 1.5 copy-start.1
  140.2 1.5 copy-start.1
  146.5 1.5 copy-start.1
  152.8 1.5 copy-start.1
where the time goes:
time: 164 us; the launch traced here: 163 us
  matrix products  98.8 us (60%)
  starting transfers between devices  35.5 us (22%)
  waiting for transfers between devices  16.8 us (10%)
  local copies, waits for them, and re-layouts  4.88 us (3%)
  other arithmetic  3.95 us (2%)
  blocking collectives  2.51 us (2%)
    dot_general x16, matrix products, one_slot(): jnp.einsum('bpn,bqn->bpq', left, panels, preferred_element_type=jnp.float32)  76.3 us
    ppermute x4, starting transfers between devices, extended(): lax.ppermute(lax.slice_in_dim(block, block.shape[dim] - width, None, axis...  27.3 us
    dot_general x16, matrix products, one_slot(): jnp.einsum('bj,jqn->bqn', picker.astype(jnp.bfloat16), ext_panels, prefer...  18.7 us
    ppermute x4, waiting for transfers between devices, extended(): lax.ppermute(lax.slice_in_dim(block, block.shape[dim] - width, None, axis...  8.47 us
    ppermute x4, waiting for transfers between devices, extended(): lax.ppermute(lax.slice_in_dim(block, 0, width, axis=dim), axis, backward)  8.35 us
    ppermute x4, starting transfers between devices, extended(): lax.ppermute(lax.slice_in_dim(block, 0, width, axis=dim), axis, backward)  8.19 us
    dot_general x16, matrix products, one_slot(): jnp.dot(picker.astype(jnp.float32), geometry, precision=lax.Precision.HIG...  3.85 us
  transfers between devices with their start and end apart: 8, of which 2 were waited for; matrix products, arithmetic and copies ran while one was open for 2% of the time, Pallas kernels for 0%

commit v1 on v0

v1 whole, which is shorter than its diff:
```python
import functools

import jax
import jax.numpy as jnp
from jax import lax
from jax.experimental import pallas as pl
from jax.experimental.pallas import tpu as pltpu
from jax.sharding import PartitionSpec as P

CHUNK = 16


def halo(block, width):
    count = lax.axis_size("row")
    forward = [(i, i + 1) for i in range(count - 1)]
    backward = [(i + 1, i) for i in range(count - 1)]
    low = lax.ppermute(block[block.shape[0] - width:], "row", forward)
    high = lax.ppermute(block[:width], "row", backward)
    return jnp.concatenate([low, block, high], axis=0)


def col_swap(x):
    return lax.ppermute(x, "col", [(0, 1), (1, 0)])


def pair_kernel(needed_ref, own_geo_ref, basis_ref, win_geo_ref, win_pan_ref, out_ref,
                bc_ref, cs_ref, *, n_off, unk, half):
    b = pl.program_id(0)
    geo = own_geo_ref[0]
    for c in range(5):
        bc_ref[c] = jnp.broadcast_to(geo[:, c:c + 1], (unk, half))

    def per_offset(o, carry):
        flag = needed_ref[b * n_off + o]

        @pl.when(flag != 0)
        def _():
            j = b + o
            wg = win_geo_ref[j]
            y0 = jnp.broadcast_to(wg[0:1, :], (CHUNK, half))
            y1 = jnp.broadcast_to(wg[1:2, :], (CHUNK, half))
            y2 = jnp.broadcast_to(wg[2:3, :], (CHUNK, half))
            sj = jnp.broadcast_to(wg[3:4, :], (CHUNK, half))
            rj = jnp.broadcast_to(wg[4:5, :], (CHUNK, half))

            def per_chunk(mc, c2):
                rows = pl.ds(pl.multiple_of(mc * CHUNK, CHUNK), CHUNK)
                d0 = bc_ref[0, rows, :] - y0
                d1 = bc_ref[1, rows, :] - y1
                d2 = bc_ref[2, rows, :] - y2
                dd = d0 * d0 + d1 * d1 + d2 * d2 + bc_ref[4, rows, :] * rj
                cv = bc_ref[3, rows, :] * sj * lax.rsqrt(dd)
                cs_ref[rows, :] = cv.astype(jnp.bfloat16)
                return c2

            lax.fori_loop(0, unk // CHUNK, per_chunk, 0, unroll=4)
            left = jnp.dot(basis_ref[0], cs_ref[...], preferred_element_type=jnp.float32)
            left = left.astype(jnp.bfloat16)
            t = lax.dot_general(left, win_pan_ref[j], (((1,), (1,)), ((), ())),
                                preferred_element_type=jnp.float32)
            out_ref[0, o] = t

        @pl.when(flag == 0)
        def _():
            out_ref[0, o] = jnp.zeros(out_ref.shape[2:], out_ref.dtype)

        return carry

    lax.fori_loop(0, n_off, per_offset, 0)


def on_device(basis, positions, seglen, radius, neighbours, counts):
    blk, half_p, unk = basis.shape
    nb_p = 2 * half_p
    half = unk // 2
    near = neighbours.shape[1]
    n_off = 2 * blk + 1
    ci = lax.axis_index("col")
    ri = lax.axis_index("row")

    other = col_swap(basis)
    own_full = jnp.where(ci == 0, jnp.concatenate([basis, other], axis=1),
                         jnp.concatenate([other, basis], axis=1))
    own_half = lax.dynamic_slice_in_dim(own_full, ci * half, half, axis=2)
    win_pan = halo(own_half, blk)

    geo = jnp.concatenate([positions, seglen[:, None, :], radius[:, None, :],
                           jnp.zeros((blk, 3, unk), jnp.float32)], axis=1)
    geo_half = lax.dynamic_slice_in_dim(geo, ci * half, half, axis=2)
    win_geo = halo(geo_half, blk)
    own_geo_t = jnp.transpose(geo, (0, 2, 1))

    own_ids = ri * blk + jnp.arange(blk, dtype=jnp.int32)
    off = jnp.clip(neighbours - own_ids[:, None] + blk, 0, 2 * blk)
    live = jnp.arange(near, dtype=jnp.int32)[None, :] < counts[:, None]
    sel = (off[:, :, None] == jnp.arange(n_off, dtype=jnp.int32)[None, None, :]) & live[:, :, None]
    needed = jnp.any(sel, axis=1).astype(jnp.int32).reshape(-1)

    kernel = functools.partial(pair_kernel, n_off=n_off, unk=unk, half=half)
    part = pl.pallas_call(
        kernel,
        out_shape=jax.ShapeDtypeStruct((blk, n_off, nb_p, nb_p), jnp.float32),
        grid_spec=pltpu.PrefetchScalarGridSpec(
            num_scalar_prefetch=1,
            grid=(blk,),
            in_specs=[
                pl.BlockSpec((1, unk, 8), lambda b, nd: (b, 0, 0)),
                pl.BlockSpec((1, nb_p, unk), lambda b, nd: (b, 0, 0)),
                pl.BlockSpec((3 * blk, 8, half), lambda b, nd: (0, 0, 0)),
                pl.BlockSpec((3 * blk, nb_p, half), lambda b, nd: (0, 0, 0)),
            ],
            out_specs=pl.BlockSpec((1, n_off, nb_p, nb_p), lambda b, nd: (b, 0, 0, 0)),
            scratch_shapes=[
                pltpu.VMEM((5, unk, half), jnp.float32),
                pltpu.VMEM((unk, half), jnp.bfloat16),
            ],
        ),
        compiler_params=pltpu.CompilerParams(dimension_semantics=("arbitrary",)),
    )(needed, own_geo_t, own_full, win_geo, win_pan)

    mine = lax.dynamic_slice_in_dim(part, ci * half_p, half_p, axis=2)
    theirs = lax.dynamic_slice_in_dim(part, (1 - ci) * half_p, half_p, axis=2)
    tiles = mine + col_swap(theirs)
    result = jnp.einsum("bko,bopq->bpkq", sel.astype(jnp.float32), tiles,
                        precision=lax.Precision.HIGHEST)
    return result.reshape(blk, half_p, near * nb_p)


def solution(mesh):
    placed = (
        P("row", "col", None),
        P("row", None, None),
        P("row", None),
        P("row", None),
        P("row", None),
        P("row"),
    )
    return jax.shard_map(
        on_device, mesh=mesh, in_specs=placed, out_specs=P("row", "col", None), check_vma=False
    )
```

time: 164 us -> 105 us (0.64)
  the two profiles are of different devices: /device:TPU:30 before, /device:TPU:65 now
where the time goes in v1:
time: 105 us
  Pallas kernels  54.1 us (52%)
  starting transfers between devices  20.7 us (20%)
  waiting for transfers between devices  12.6 us (12%)
  local copies, waits for them, and re-layouts  8.45 us (8%)
  other arithmetic  6.71 us (6%)
  matrix products  2.57 us (2%)
    pallas_call x1, Pallas kernels, on_device(): pl.pallas_call(kernel, out_shape=jax.ShapeDtypeStruct((blk, n_off, nb_p,...  54.1 us
    ppermute x2, starting transfers between devices, halo(): high = lax.ppermute(block[:width], 'row', backward)  14.2 us
    ppermute x2, waiting for transfers between devices, halo(): low = lax.ppermute(block[block.shape[0] - width:], 'row', forward)  7.86 us
    ppermute x2, waiting for transfers between devices, col_swap(): return lax.ppermute(x, 'col', [(0, 1), (1, 0)])  4.71 us
    ppermute x2, starting transfers between devices, halo(): low = lax.ppermute(block[block.shape[0] - width:], 'row', forward)  3.84 us
    add x1, other arithmetic, on_device(): tiles = mine + col_swap(theirs)  2.83 us
    ppermute x2, starting transfers between devices, col_swap(): return lax.ppermute(x, 'col', [(0, 1), (1, 0)])  2.63 us
    dot_general x1, matrix products, on_device(): jnp.einsum('bko,bopq->bpkq', sel.astype(jnp.float32), tiles, precision=la...  2.57 us
  transfers between devices with their start and end apart: 6, of which 3 were waited for; matrix products, arithmetic and copies ran while one was open for 5% of the time, Pallas kernels for 0%

profile of v1, /device:TPU:65, one launch (start us, length us, event | category | flops | bytes accessed | tf_op | source)
XLA Modules:
  0.0 105.3 jit_solution(3737090305650719403)
XLA Ops:
  0.0 0.0 copy-start.1
  0.0 0.7 broadcast_in_dim.6
  0.7 0.7 broadcast_in_dim.7
  1.5 0.8 copy.7
  2.3 0.1 pad.13.clone
  2.4 0.1 maximum_maximum_fusion
  2.5 6.4 %collective-permute-start.2 = (f32[8,8,256]{2,1,0:T(8,128)S(1)}, f32[8,8,256]{2,1,0:T(8,128)S(1)}, u32[]{:S(2)}, u32[]{:S(2)}) collective-permute-start(f32[8,8,256]{2,1,0:T(8,128)S(1)} %constant_dynamic-slice_fusion.2), channel_id=1, source_target_pairs={{2,0},{4,2},{6,4},{8,6},{10,8},{12,10},{14,12},{16,14},{18,16},{20... | collective-permute-start | bytes 196616 | tf_op jit(solution)/shard_map/ppermute | solution.py:18
  8.9 1.9 %collective-permute-start.1 = (f32[8,8,256]{2,1,0:T(8,128)S(1)}, f32[8,8,256]{2,1,0:T(8,128)S(1)}, u32[]{:S(2)}, u32[]{:S(2)}) collective-permute-start(f32[8,8,256]{2,1,0:T(8,128)S(1)} %constant_dynamic-slice_fusion.2), channel_id=1, source_target_pairs={{0,2},{2,4},{4,6},{6,8},{8,10},{10,12},{12,14},{14,16},{16,18},{18... | collective-permute-start | bytes 196616 | tf_op jit(solution)/shard_map/ppermute | solution.py:17
  10.8 1.0 collective-permute-start
  11.9 0.8 add_clamp_fusion
  12.6 0.6 collective-permute-done
  13.3 1.2 %maximum_select_fusion.basis_ref = bf16[8,64,512]{2,1,0:T(8,128)(2,1)S(1)} fusion(bf16[8,32,512]{2,1,0:T(8,128)(2,1)S(1)} %collective-permute-done, bf16[8,32,512]{2,1,0:T(8,128)(2,1)} %param.6, pred[]{:T(512)S(6)} %eq.19), kind=kLoop, calls=%fused_computation.5 | loop fusion | flops 2359296 | bytes 1048577 | tf_op jit(solution)/shard_map/jit(_where)/select_n | solution.py:82
  14.4 0.0 copy-start
  14.5 7.9 %collective-permute-start.4 = (bf16[8,64,256]{2,1,0:T(8,128)(2,1)S(1)}, bf16[8,64,256]{2,1,0:T(8,128)(2,1)S(1)}, u32[]{:S(2)}, u32[]{:S(2)}) collective-permute-start(bf16[8,64,256]{2,1,0:T(8,128)(2,1)S(1)} %constant_dynamic-slice_fusion.1), channel_id=1, source_target_pairs={{2,0},{4,2},{6,4},{8,6},{10,8},{12,10},{14,12},{16,14},{18,16},{20... | collective-permute-start | bytes 786440 | tf_op jit(solution)/shard_map/ppermute | solution.py:18
  22.3 1.9 %collective-permute-start.3 = (bf16[8,64,256]{2,1,0:T(8,128)(2,1)S(1)}, bf16[8,64,256]{2,1,0:T(8,128)(2,1)S(1)}, u32[]{:S(2)}, u32[]{:S(2)}) collective-permute-start(bf16[8,64,256]{2,1,0:T(8,128)(2,1)S(1)} %constant_dynamic-slice_fusion.1), channel_id=1, source_target_pairs={{0,2},{2,4},{4,6},{6,8},{8,10},{10,12},{12,14},{14,16},{16,18},{18... | collective-permute-start | bytes 786440 | tf_op jit(solution)/shard_map/ppermute | solution.py:17
  24.3 0.0 copy-done.1
  24.3 0.1 iota_compare_fusion.1
  24.4 0.1 fusion.7
  24.5 0.7 reshape.34.needed_ref
  25.1 2.0 %copy.8.own_geo_ref = f32[8,512,8]{2,1,0:T(8,128)} copy(f32[8,512,8]{1,2,0:T(8,128)S(1)} %get-tuple-element.6) | data formatting | bytes 262144 | tf_op jit(solution)/shard_map/transpose | solution.py:91
  27.1 0.0 collective-permute-done.2
  27.1 0.0 collective-permute-done.1
  27.1 0.7 pad_maximum_fusion.1.win_geo_ref
  27.8 0.0 collective-permute-done.4
  27.8 7.9 %collective-permute-done.3 = bf16[8,64,256]{2,1,0:T(8,128)(2,1)S(1)} collective-permute-done((bf16[8,64,256]{2,1,0:T(8,128)(2,1)S(1)}, bf16[8,64,256]{2,1,0:T(8,128)(2,1)S(1)}, u32[]{:S(2)}, u32[]{:S(2)}) %collective-permute-start.3) | collective-permute-done | bytes 262176 | tf_op jit(solution)/shard_map/ppermute | solution.py:17
  35.7 1.0 pad_maximum_fusion.win_pan_ref
  36.6 0.0 copy-done
  36.6 54.1 %shard_map.64 = f32[8,17,64,64]{3,2,1,0:T(8,128)} custom-call(s32[136]{0:T(256)} %reshape.34.needed_ref, f32[8,512,8]{2,1,0:T(8,128)} %copy.8.own_geo_ref, bf16[8,64,512]{2,1,0:T(8,128)(2,1)} %copy-done, f32[24,8,256]{2,1,0:T(8,128)} %pad_maximum_fusion.1.win_geo_ref, bf16[24,64,256]{2,1,0:T(8,128)(2,1)} %pad_maximum_fusion.win_pan_ref), custom_call_target="tpu_custom_call" | custom-call | tf_op jit(solution)/shard_map/pallas_call | solution.py:100
  90.7 1.9 %constant_dynamic-slice_fusion = f32[8,17,32,64]{3,2,1,0:T(8,128)S(1)} fusion(f32[8,17,64,64]{3,2,1,0:T(8,128)} %shard_map.64, s32[]{:T(128)S(6)} %select_n.22), kind=kLoop, calls=%fused_computation.16 | loop fusion | bytes 2228228 | tf_op jit(solution)/shard_map/dynamic_slice | solution.py:122
  92.6 1.6 %collective-permute-start.5 = (f32[8,17,32,64]{3,2,1,0:T(8,128)S(1)}, f32[8,17,32,64]{3,2,1,0:T(8,128)}, u32[]{:S(2)}, u32[]{:S(2)}) collective-permute-start(f32[8,17,32,64]{3,2,1,0:T(8,128)S(1)} %constant_dynamic-slice_fusion), channel_id=1, source_target_pairs={{0,1},{1,0},{2,3},{3,2},{4,5},{5,4},{6,7},{7,6},{8,9},{9,8},{10,11... | collective-permute-start | bytes 3342344 | tf_op jit(solution)/shard_map/ppermute | solution.py:23
  94.2 4.1 %collective-permute-done.5 = f32[8,17,32,64]{3,2,1,0:T(8,128)} collective-permute-done((f32[8,17,32,64]{3,2,1,0:T(8,128)S(1)}, f32[8,17,32,64]{3,2,1,0:T(8,128)}, u32[]{:S(2)}, u32[]{:S(2)}) %collective-permute-start.5) | collective-permute-done | bytes 1114144 | tf_op jit(solution)/shard_map/ppermute | solution.py:23
  98.3 2.8 %dynamic-slice_add_fusion = f32[8,17,32,64]{3,2,1,0:T(8,128)S(1)} fusion(f32[8,17,32,64]{3,2,1,0:T(8,128)} %collective-permute-done.5, f32[8,17,64,64]{3,2,1,0:T(8,128)} %shard_map.64, s32[]{:T(128)S(6)} %select_n.21), kind=kLoop, calls=%fused_computation.2 | loop fusion | flops 278528 | bytes 3342340 | tf_op jit(solution)/shard_map/add | solution.py:123
  101.1 2.6 %fusion.2 = f32[8,32,16,64]{3,2,1,0:T(8,128)S(1)} fusion(f32[8,17,32,64]{3,2,1,0:T(8,128)S(1)} %dynamic-slice_add_fusion, s32[8,16]{1,0:T(8,128)S(1)} %add_clamp_fusion, pred[8,16]{1,0:T(8,128)(4,1)S(1)} %iota_compare_fusion.1), kind=kOutput, calls=%fused_computation.3 | convolution fusion | flops 53481728 | bytes 2163328 | tf_op jit(solution)/shard_map/bko,bopq->bpkq/dot_general | solution.py:124
  103.7 1.5 %reshape.33 = f32[8,32,1024]{2,1,0:T(8,128)} reshape(f32[8,32,16,64]{3,2,1,0:T(8,128)S(1)} %fusion.2) | data formatting | bytes 2097152 | tf_op jit(solution)/shard_map/reshape | solution.py:126
  (5 shorter events, 0.1 us)
Async XLA Ops:
  0.0 24.3 %copy-start.1 = (s32[8]{0:T(128)S(1)}, s32[8]{0:T(128)}, u32[]{:S(2)}) copy-start(s32[8]{0:T(128)} %param.11) | copy-start | bytes 100
  2.5 24.6 %collective-permute-start.2 = (f32[8,8,256]{2,1,0:T(8,128)S(1)}, f32[8,8,256]{2,1,0:T(8,128)S(1)}, u32[]{:S(2)}, u32[]{:S(2)}) collective-permute-start(f32[8,8,256]{2,1,0:T(8,128)S(1)} %constant_dynamic-slice_fusion.2), channel_id=1, source_target_pairs={{2,0},{4,2},{6,4},{8,6},{10,8},{12,10},{14,12},{16,14},{18,16},{20... | collective-permute-start | bytes 196616 | tf_op jit(solution)/shard_map/ppermute | solution.py:18
  8.9 18.2 %collective-permute-start.1 = (f32[8,8,256]{2,1,0:T(8,128)S(1)}, f32[8,8,256]{2,1,0:T(8,128)S(1)}, u32[]{:S(2)}, u32[]{:S(2)}) collective-permute-start(f32[8,8,256]{2,1,0:T(8,128)S(1)} %constant_dynamic-slice_fusion.2), channel_id=1, source_target_pairs={{0,2},{2,4},{4,6},{6,8},{8,10},{10,12},{12,14},{14,16},{16,18},{18... | collective-permute-start | bytes 196616 | tf_op jit(solution)/shard_map/ppermute | solution.py:17
  10.8 2.4 %collective-permute-start = (bf16[8,32,512]{2,1,0:T(8,128)(2,1)}, bf16[8,32,512]{2,1,0:T(8,128)(2,1)S(1)}, u32[]{:S(2)}, u32[]{:S(2)}) collective-permute-start(bf16[8,32,512]{2,1,0:T(8,128)(2,1)} %param.6), channel_id=1, source_target_pairs={{0,1},{1,0},{2,3},{3,2},{4,5},{5,4},{6,7},{7,6},{8,9},{9,8},{10,11... | collective-permute-start | bytes 786440 | tf_op jit(solution)/shard_map/ppermute | solution.py:23
  14.4 22.2 %copy-start = (bf16[8,64,512]{2,1,0:T(8,128)(2,1)}, bf16[8,64,512]{2,1,0:T(8,128)(2,1)S(1)}, u32[]{:S(2)}) copy-start(bf16[8,64,512]{2,1,0:T(8,128)(2,1)S(1)} %maximum_select_fusion.basis_ref) | copy-start | bytes 1572868
  14.5 13.3 %collective-permute-start.4 = (bf16[8,64,256]{2,1,0:T(8,128)(2,1)S(1)}, bf16[8,64,256]{2,1,0:T(8,128)(2,1)S(1)}, u32[]{:S(2)}, u32[]{:S(2)}) collective-permute-start(bf16[8,64,256]{2,1,0:T(8,128)(2,1)S(1)} %constant_dynamic-slice_fusion.1), channel_id=1, source_target_pairs={{2,0},{4,2},{6,4},{8,6},{10,8},{12,10},{14,12},{16,14},{18,16},{20... | collective-permute-start | bytes 786440 | tf_op jit(solution)/shard_map/ppermute | solution.py:18
  22.3 13.3 %collective-permute-start.3 = (bf16[8,64,256]{2,1,0:T(8,128)(2,1)S(1)}, bf16[8,64,256]{2,1,0:T(8,128)(2,1)S(1)}, u32[]{:S(2)}, u32[]{:S(2)}) collective-permute-start(bf16[8,64,256]{2,1,0:T(8,128)(2,1)S(1)} %constant_dynamic-slice_fusion.1), channel_id=1, source_target_pairs={{0,2},{2,4},{4,6},{6,8},{8,10},{10,12},{12,14},{14,16},{16,18},{18... | collective-permute-start | bytes 786440 | tf_op jit(solution)/shard_map/ppermute | solution.py:17
  92.6 5.7 %collective-permute-start.5 = (f32[8,17,32,64]{3,2,1,0:T(8,128)S(1)}, f32[8,17,32,64]{3,2,1,0:T(8,128)}, u32[]{:S(2)}, u32[]{:S(2)}) collective-permute-start(f32[8,17,32,64]{3,2,1,0:T(8,128)S(1)} %constant_dynamic-slice_fusion), channel_id=1, source_target_pairs={{0,1},{1,0},{2,3},{3,2},{4,5},{5,4},{6,7},{7,6},{8,9},{9,8},{10,11... | collective-permute-start | bytes 3342344 | tf_op jit(solution)/shard_map/ppermute | solution.py:23
